TPU v7x, 512 devices: a whole 4x4x16 slice. The times are simulated.
512 devices in a mesh: req: 32 (over y, x, core), grp: 16 (over z).
Axes of the slice: x: 4, y: 4, z: 16, core: 2. Of those that a mesh axis runs over, the one named last changes fastest.
Arguments:
- normed_token_input: bfloat16 [256, 8192], P(None, 'req'), may hold values from -6 to 6
- key_value_weight: bfloat16 [8192, 2048], P('req', 'grp'), may hold values from -0.0625 to 0.0625
- adapter_down_weight: bfloat16 [8192, 128, 128], P('req', 'grp'), may hold values from -0.0625 to 0.0625
- adapter_up_weight: bfloat16 [128, 64, 2048], P(None, None, 'grp'), may hold values from -0.75 to 0.75
- adapter_index_rows: int32 [256, 1], replicated, may hold values from 0 to 127
- queries: bfloat16 [256, 8192], P('req')
- key_value_pages: bfloat16 [10240, 16, 2, 8, 128], P('req', 'grp')
- lengths: int32 [256], P('req'), may hold values from 0 to 511, as said below
- page_slot_table: int32 [256, 32], P('req'), may hold values from 0 to 255, as said below
- departing_slots: int32 [1024], P('req'), may hold values from 0 to 255, as said below
- departing_target: int32 [1024, 1], P('req'), may hold values from 0 to 31; in each aligned block of 32 rows (0 to 31, 32 to 63, ...) at most 2 rows name the same one
Outputs:
- attention: bfloat16 [256, 8192], P('req')
- migrated_pool: bfloat16 [10240, 16, 2, 8, 128], P('req', 'grp')
Inputs may be any that keep to these rules, and one draw needn't show every extreme that they name: `adapter_index_rows`: each row names one adapter; every adapter is named by some request. `lengths`: some request has an empty cache and some has 511 cached tokens. `page_slot_table`: the rows of the requests of one home together name each of that home's slots 0 .. 255 exactly once. `departing_slots`: the 32 entries of one home are distinct. `departing_target`: the 32 rows of one home name one target at most 2 times; some home names some target exactly 2 times.
All inputs are finite; a program needn't handle non-finite values.
Results may differ from a plain program's by a relative error of at most 0.01345.
Values may be sent and summed in bfloat16 or wider, within the bound.
No kernel may reach another device: no remote copies, remote signals or barrier semaphores. Data moves between devices by JAX's collectives and lax.ppermute only.
A program may use at most 64 MiB of HBM per device.

v0:
```python
import math
import jax
import jax.numpy as jnp
from jax import lax
from jax.sharding import PartitionSpec as P

adapter_scale = 2.0
masked_score = -1e30


def shards(
    normed_token_input,
    key_value_weight,
    adapter_down_weight,
    adapter_up_weight,
    adapter_index_rows,
    queries,
    key_value_pages,
    lengths,
    page_slot_table,
    departing_slots,
    departing_target,
):
    selected_adapter = adapter_index_rows[:, 0]
    homes = lax.axis_size("req")
    groups = lax.axis_size("grp")
    home_index = lax.axis_index("req")
    group_index = lax.axis_index("grp")
    rows = lengths.shape[0]
    request_count = normed_token_input.shape[0]
    column_span = key_value_weight.shape[1]
    local_adapters = adapter_down_weight.shape[1]
    rank_width = adapter_down_weight.shape[2]
    rank_half = adapter_up_weight.shape[1]
    slot_tokens = key_value_pages.shape[1]
    heads = key_value_pages.shape[3]
    head_dim = key_value_pages.shape[4]
    key_width = heads * head_dim
    query_heads = queries.shape[1] // head_dim
    heads_per_target = query_heads // groups
    page_size = slot_tokens * groups
    pages = page_slot_table.shape[1]
    both = jnp.concatenate(
        [key_value_weight, adapter_down_weight.reshape(adapter_down_weight.shape[0], -1)], axis=1
    )
    products = jnp.dot(normed_token_input, both, preferred_element_type=jnp.float32)
    base_part = products[:, :column_span]
    down_all = products[:, column_span:].reshape(request_count, local_adapters, rank_width)
    local_choice = selected_adapter - group_index * local_adapters
    picker = (local_choice[:, None] == jnp.arange(local_adapters, dtype=jnp.int32)[None, :]).astype(
        jnp.float32
    )
    mid_part = jnp.einsum("ia,iaw->iw", picker, down_all)
    partial = jnp.concatenate([base_part, mid_part], axis=1).reshape(homes, rows, -1)
    summed = jnp.sum(lax.all_to_all(partial, "req", 0, 0, tiled=False), axis=0)
    base_resident = summed[:, :column_span]
    mid_owned = summed[:, column_span:].astype(jnp.bfloat16)
    resident_adapters = lax.dynamic_slice_in_dim(selected_adapter, home_index * rows, rows)
    owner = resident_adapters // local_adapters
    mid_spread = lax.all_to_all(
        jnp.broadcast_to(mid_owned[None], (groups,) + mid_owned.shape), "grp", 0, 0, tiled=False
    )
    request_index = jnp.arange(rows, dtype=jnp.int32)
    mid_home = mid_spread[owner, request_index]
    is_value = group_index * column_span >= key_width
    mid_used = jnp.where(is_value, mid_home[:, rank_half:], mid_home[:, :rank_half])
    up_weight_rows = adapter_up_weight[resident_adapters]
    adapter_update = jnp.einsum(
        "ir,irc->ic", mid_used, up_weight_rows, preferred_element_type=jnp.float32
    )
    fresh_columns = (base_resident + adapter_scale * adapter_update).astype(jnp.bfloat16)
    gathered = key_value_pages[page_slot_table][:, :, 0]
    keys = gathered[:, :, 0]
    values = gathered[:, :, 1]
    query = queries.reshape(rows, heads, -1, head_dim)
    scores = jnp.einsum(
        "ihgd,inhd->ihgn", query, keys, preferred_element_type=jnp.float32
    ) / math.sqrt(head_dim)
    positions = jnp.arange(pages, dtype=jnp.int32) * page_size + group_index * slot_tokens
    valid = (positions[None, :] < lengths[:, None])[:, None, None, :]
    scores = jnp.where(valid, scores, masked_score)
    local_top = jnp.max(scores, axis=3)
    weights = jnp.where(valid, jnp.exp(scores - local_top[..., None]), 0.0)
    local_total = jnp.sum(weights, axis=3)
    local_mixed = jnp.einsum("ihgn,inhd->ihgd", weights, values, preferred_element_type=jnp.float32)
    parcel = jnp.concatenate(
        [
            local_mixed.reshape(rows, groups, heads_per_target * head_dim),
            local_top.reshape(rows, groups, heads_per_target),
            local_total.reshape(rows, groups, heads_per_target),
            jnp.broadcast_to(
                fresh_columns.astype(jnp.float32)[:, None, :], (rows, groups, column_span)
            ),
        ],
        axis=2,
    ).transpose(1, 0, 2)
    received = lax.all_to_all(parcel, "grp", 0, 0, tiled=False)
    mixed_width = heads_per_target * head_dim
    shard_mixed = received[:, :, :mixed_width].reshape(groups, rows, heads_per_target, head_dim)
    shard_top = received[:, :, mixed_width : mixed_width + heads_per_target]
    shard_total = received[
        :, :, mixed_width + heads_per_target : mixed_width + 2 * heads_per_target
    ]
    new_all = received[:, :, mixed_width + 2 * heads_per_target :].astype(jnp.bfloat16)
    new_all = new_all.transpose(1, 0, 2).reshape(rows, groups * column_span)
    new_keys = new_all[:, :key_width].reshape(rows, heads, head_dim)
    new_values = new_all[:, key_width:].reshape(rows, heads, head_dim)
    head_of_target = group_index * heads_per_target // (query_heads // heads)
    own_query = lax.dynamic_slice_in_dim(
        queries, group_index * mixed_width, mixed_width, axis=1
    ).reshape(rows, heads_per_target, head_dim)
    own_key = lax.dynamic_index_in_dim(new_keys, head_of_target, 1, False)
    own_value = lax.dynamic_index_in_dim(new_values, head_of_target, 1, False)
    new_score = jnp.einsum(
        "ihd,id->ih", own_query, own_key, preferred_element_type=jnp.float32
    ) / math.sqrt(head_dim)
    top = jnp.maximum(jnp.max(shard_top, axis=0), new_score)
    shard_scale = jnp.exp(shard_top - top[None])
    new_weight = jnp.exp(new_score - top)
    total = jnp.sum(shard_total * shard_scale, axis=0) + new_weight
    mixed = (
        jnp.sum(shard_mixed * shard_scale[..., None], axis=0)
        + new_weight[..., None] * own_value.astype(jnp.float32)[:, None, :]
    )
    own_attention = (mixed / total[..., None]).astype(jnp.bfloat16).reshape(rows, mixed_width)
    attention = lax.all_gather(own_attention, "grp", axis=1, tiled=True)
    page_slot = page_slot_table[request_index, lengths // page_size]
    offset = lengths % page_size
    mine = offset // slot_tokens == group_index
    token_local = offset % slot_tokens
    current = key_value_pages[page_slot, token_local]
    fresh = jnp.stack([new_keys, new_values], axis=1)
    written = key_value_pages.at[page_slot, token_local].set(
        jnp.where(mine[:, None, None, None], fresh, current)
    )
    targets = departing_target[:, 0]
    count_out = departing_slots.shape[0]
    order = jnp.arange(count_out, dtype=jnp.int32)
    earlier = (targets[:, None] == targets[None, :]) & (order[None, :] < order[:, None])
    place = jnp.sum(earlier.astype(jnp.int32), axis=1)
    live_slots = rows * pages
    capacity = (key_value_pages.shape[0] - live_slots) // homes
    outbound = (
        jnp.zeros((homes, capacity) + key_value_pages.shape[1:], key_value_pages.dtype)
        .at[targets, place]
        .set(written[departing_slots])
    )
    arrived = lax.all_to_all(outbound, "req", split_axis=0, concat_axis=0, tiled=True)
    migrated_pool = jnp.concatenate(
        [written[:live_slots], arrived.reshape((homes * capacity,) + key_value_pages.shape[1:])],
        axis=0,
    )
    return (attention, migrated_pool)


def solution(mesh):
    in_specs = (
        P(None, "req"),
        P("req", "grp"),
        P("req", "grp", None),
        P(None, None, "grp"),
        P(),
        P("req", None),
        P("req", "grp", None, None, None),
        P("req"),
        P("req", None),
        P("req"),
        P("req", None),
    )
    out_specs = (P("req", None), P("req", "grp", None, None, None))
    return jax.shard_map(shards, mesh=mesh, in_specs=in_specs, out_specs=out_specs, check_vma=False)
```

profile of v0, /device:TPU:1, one launch (start us, length us, event | category | flops | bytes accessed | tf_op | source)
XLA Modules:
  0.0 158.4 jit_solution(13711185269570245694)
XLA Ops:
  0.7 1.5 copy.92
  5.8 1.3 multiply_reduce_fusion
  7.9 1.8 %copy.43 = f32[256,256]{1,0:T(8,128)} copy(f32[256,256]{0,1:T(8,128)} %pad_maximum_fusion.1) | data formatting | bytes 524288 | tf_op jit(solution)/shard_map/concatenate | solution.py:54
  9.7 11.0 %all-to-all-start = ((f32[32,8,256]{2,1,0:T(8,128)}), f32[32,8,256]{2,1,0:T(8,128)}, u32[]{:S(2)}, u32[]{:S(2)}) async-start(f32[32,8,256]{2,1,0:T(8,128)} %bitcast.113), calls=%async_computation | async-start | bytes 524288 | tf_op jit(solution)/shard_map/all_to_all | solution.py:55
  20.8 1.8 %gather_fusion = bf16[256,2,8,128]{3,2,1,0:T(8,128)(2,1)} fusion(bf16[320,2,8,128]{3,2,1,0:T(8,128)(2,1)S(1)} %bitcast.107, s32[1024]{0:T(1024)S(1)} %pad_clamp_fusion.2), kind=kCustom, calls=%fused_computation | custom fusion | bytes 2098176 | tf_op jit(solution)/shard_map/gather | solution.py:72
  22.6 2.1 %fusion.41 = (bf16[8,32,1,8,128]{4,3,2,1,0:T(8,128)(2,1)}, bf16[8,32,1,8,128]{4,3,2,1,0:T(8,128)(2,1)S(1)}) fusion(bf16[8,32,2,8,128]{4,3,2,1,0:T(8,128)(2,1)} %bitcast.110), kind=kLoop, calls=%fused_computation.114 | loop fusion | bytes 2097152 | tf_op jit(solution)/shard_map/slice | solution.py:74
  26.2 2.1 %fusion.5 = f32[8,8,8,128]{3,2,1,0:T(8,128)} fusion(bf16[8,32,1,8,128]{4,3,2,1,0:T(8,128)(2,1)} %get-tuple-element.6, f32[8,8,8,32]{3,2,1,0:T(8,128)} %copy-done.3, f32[8,8,8]{2,1,0:T(8,128)S(1)} %get-tuple-element.16, pred[8,32]{1,0:T(8,128)(4,1)S(1)} %broadcast_compare_fusion), kind=kOutput, calls=%fused_computation.20 | convolution fusion | flops 4227072 | bytes 854272 | tf_op jit(solution)/shard_map/ihgn,inhd->ihgd/dot_general | solution.py:85
  28.4 1.4 all-to-all-done
  31.4 12.5 %all-to-all-start.1 = ((bf16[16,8,128]{2,1,0:T(8,128)(2,1)}), bf16[16,8,128]{2,1,0:T(8,128)(2,1)}, u32[]{:S(2)}, u32[]{:S(2)}) async-start(bf16[16,8,128]{2,1,0:T(8,128)(2,1)} %broadcast_in_dim.45), calls=%async_computation.1 | async-start | bytes 65536 | tf_op jit(solution)/shard_map/all_to_all | solution.py:60
  46.4 1.7 %reshape.115 = f32[8,16,512]{2,1,0:T(8,128)} reshape(f32[8,8,8,128]{3,2,1,0:T(8,128)} %fusion.5) | data formatting | bytes 524288 | tf_op jit(solution)/shard_map/reshape | solution.py:88
  48.0 1.8 %copy.44 = f32[8,16,512]{2,0,1:T(8,128)} copy(f32[8,16,512]{2,1,0:T(8,128)} %reshape.115) | data formatting | bytes 524288 | tf_op jit(solution)/shard_map/reshape | solution.py:88
  49.8 1.2 pad_clamp_fusion.1
  51.1 1.3 gather_fusion.2
  52.4 3.1 %all-to-all-done.1 = bf16[16,8,128]{2,1,0:T(8,128)(2,1)} async-done(((bf16[16,8,128]{2,1,0:T(8,128)(2,1)}), bf16[16,8,128]{2,1,0:T(8,128)(2,1)}, u32[]{:S(2)}, u32[]{:S(2)}) %all-to-all-start.1) | async-done | bytes 32800 | tf_op jit(solution)/shard_map/all_to_all | solution.py:60
  55.5 1.9 %gather_fusion.1 = bf16[8,128]{1,0:T(8,128)(2,1)} fusion(bf16[16,8,128]{2,1,0:T(8,128)(2,1)} %all-to-all-done.1, s32[8]{0:T(128)S(1)} %get-tuple-element.12), kind=kCustom, calls=%fused_computation.1 | custom fusion | bytes 4160 | tf_op jit(solution)/shard_map/gather | solution.py:64
  59.3 1.8 %maximum_bitcast_fusion = f32[16,8,648]{2,1,0:T(8,128)} fusion(f32[8,16,128]{2,0,1:T(8,128)S(1)} %broadcast_in_dim.46, f32[8,16,4]{2,0,1:T(8,128)S(1)} %copy.46, f32[8,16,4]{2,0,1:T(8,128)S(1)} %copy.45, f32[8,16,512]{2,0,1:T(8,128)} %copy.44), kind=kLoop, calls=%fused_computation.22 | loop fusion | flops 248832 | bytes 663552 | tf_op jit(solution)/shard_map/transpose | solution.py:96
  61.1 8.4 %all-to-all-start.2 = ((f32[16,8,648]{2,1,0:T(8,128)}), f32[16,8,648]{2,1,0:T(8,128)}, u32[]{:S(2)}, u32[]{:S(2)}) async-start(f32[16,8,648]{2,1,0:T(8,128)} %maximum_bitcast_fusion), calls=%async_computation.2 | async-start | bytes 786432 | tf_op jit(solution)/shard_map/all_to_all | solution.py:97
  74.9 1.2 fusion.26
  76.7 10.9 %all-to-all-done.2 = f32[16,8,648]{2,1,0:T(8,128)} async-done(((f32[16,8,648]{2,1,0:T(8,128)}), f32[16,8,648]{2,1,0:T(8,128)}, u32[]{:S(2)}, u32[]{:S(2)}) %all-to-all-start.2) | async-done | bytes 331808 | tf_op jit(solution)/shard_map/all_to_all | solution.py:97
  93.5 28.5 %all_gather.3 = bf16[8,8192]{1,0:T(8,128)(2,1)} all-gather(bf16[8,512]{1,0:T(8,128)(2,1)S(1)} %fusion.15), channel_id=1, replica_groups=mesh['req'=32,'grp'=16] {'grp'}, dimensions={1}, use_global_device_ids=true | all-gather | bytes 139264 | tf_op jit(solution)/shard_map/all_gather | solution.py:126
  125.7 3.8 %scatter_fusion.1 = bf16[32,2,2,8,128]{4,3,2,1,0:T(8,128)(2,1)} fusion(bf16[32,2,2,8,128]{4,3,2,1,0:T(8,128)(2,1)} %broadcast.228, s32[32]{0:T(128)S(1)} %fusion.36, bf16[32,2,8,128]{3,2,1,0:T(8,128)(2,1)S(1)} %gather_fusion.5), kind=kCustom, calls=%fused_computation.7 | custom fusion | bytes 393472 | tf_op jit(solution)/shard_map/scatter | solution.py:146
  129.5 16.8 %all-to-all-start.3 = ((bf16[32,2,1,2,8,128]{5,4,3,1,2,0:T(8,128)(2,1)}), bf16[32,2,1,2,8,128]{5,4,3,1,2,0:T(8,128)(2,1)}, u32[]{:S(2)}, u32[]{:S(2)}) async-start(bf16[32,2,1,2,8,128]{5,4,3,1,2,0:T(8,128)(2,1)} %bitcast.112), calls=%async_computation.3 | async-start | bytes 524288 | tf_op jit(solution)/shard_map/all_to_all | solution.py:148
  147.4 7.8 %all-to-all-done.3 = bf16[32,2,1,2,8,128]{5,4,3,1,2,0:T(8,128)(2,1)} async-done(((bf16[32,2,1,2,8,128]{5,4,3,1,2,0:T(8,128)(2,1)}), bf16[32,2,1,2,8,128]{5,4,3,1,2,0:T(8,128)(2,1)}, u32[]{:S(2)}, u32[]{:S(2)}) %all-to-all-start.3) | async-done | bytes 262176 | tf_op jit(solution)/shard_map/all_to_all | solution.py:148
  155.2 2.5 %pad_maximum_fusion = bf16[320,1,2,8,128]{4,3,2,1,0:T(8,128)(2,1)} fusion(bf16[64,1,2,8,128]{4,3,2,1,0:T(8,128)(2,1)} %bitcast.43, bf16[256,1,2,8,128]{4,3,2,1,0:T(8,128)(2,1)} %slice_bitcast_fusion), kind=kLoop, calls=%fused_computation.9 | loop fusion | flops 655360 | bytes 2621440 | tf_op jit(solution)/shard_map/concatenate | solution.py:149
  (82 shorter events, 29.3 us)
Async XLA Ops:
  0.6 50.4 %copy-start = (bf16[128,64,128]{2,1,0:T(8,128)(2,1)S(1)}, bf16[128,64,128]{2,1,0:T(8,128)(2,1)}, u32[]{:S(2)}) copy-start(bf16[128,64,128]{2,1,0:T(8,128)(2,1)} %param.14) | copy-start | bytes 6291460
  0.6 1.7 %copy-start.6 = (bf16[256,256]{1,0:T(8,128)(2,1)S(1)}, bf16[256,256]{1,0:T(8,128)(2,1)}, u32[]{:S(2)}) copy-start(bf16[256,256]{1,0:T(8,128)(2,1)} %param.11) | copy-start | bytes 393220
  0.7 1.7 %copy-start.7 = (bf16[256,128]{1,0:T(8,128)(2,1)S(1)}, bf16[256,128]{1,0:T(8,128)(2,1)}, u32[]{:S(2)}) copy-start(bf16[256,128]{1,0:T(8,128)(2,1)} %param.12) | copy-start | bytes 196612
  0.7 1.6 %copy-start.4 = (bf16[256,8,128]{2,1,0:T(8,128)(2,1)S(1)}, bf16[256,8,128]{2,1,0:T(8,128)(2,1)}, u32[]{:S(2)}) copy-start(bf16[256,8,128]{2,1,0:T(8,128)(2,1)} %param.13) | copy-start | bytes 1572868
  2.7 1.4 copy-start.2
  2.8 1.4 copy-start.8
  4.1 3.1 %slice-start = ((f32[256,1152]{0,1:T(8,128)}), f32[256,128]{0,1:T(8,128)S(1)}, s32[]{:S(2)}) async-start(f32[256,1152]{0,1:T(8,128)} %copy-done.2), calls=%async_computation.4 | async-start | bytes 262144 | tf_op jit(solution)/shard_map/slice | solution.py:47
  5.8 14.9 %copy-start.1 = (s32[8,32]{1,0:T(8,128)S(1)}, s32[8,32]{1,0:T(8,128)}, u32[]{:S(2)}) copy-start(s32[8,32]{1,0:T(8,128)} %param.19) | copy-start | bytes 3076
  9.7 20.1 %all-to-all-start = ((f32[32,8,256]{2,1,0:T(8,128)}), f32[32,8,256]{2,1,0:T(8,128)}, u32[]{:S(2)}, u32[]{:S(2)}) async-start(f32[32,8,256]{2,1,0:T(8,128)} %bitcast.113), calls=%async_computation | async-start | bytes 524288 | tf_op jit(solution)/shard_map/all_to_all | solution.py:55
  22.6 2.1 %copy-start.11 = (s32[8]{0:T(128)S(1)}, s32[8]{0:T(128)}, u32[]{:S(2)}) copy-start(s32[8]{0:T(128)} %param.18) | copy-start | bytes 100
  22.6 2.2 %copy-start.10 = (bf16[8,8192]{1,0:T(8,128)(2,1)S(1)}, bf16[8,8192]{1,0:T(8,128)(2,1)}, u32[]{:S(2)}) copy-start(bf16[8,8192]{1,0:T(8,128)(2,1)} %param.16) | copy-start | bytes 393220
  24.8 19.1 %copy-start.9 = (s32[256,1]{0,1:T(1,128)S(1)}, s32[256,1]{0,1:T(1,128)}, u32[]{:S(2)}) copy-start(s32[256,1]{0,1:T(1,128)} %param.15) | copy-start | bytes 3076
  25.3 0.7 copy-start.3
  31.4 24.1 %all-to-all-start.1 = ((bf16[16,8,128]{2,1,0:T(8,128)(2,1)}), bf16[16,8,128]{2,1,0:T(8,128)(2,1)}, u32[]{:S(2)}, u32[]{:S(2)}) async-start(bf16[16,8,128]{2,1,0:T(8,128)(2,1)} %broadcast_in_dim.45), calls=%async_computation.1 | async-start | bytes 65536 | tf_op jit(solution)/shard_map/all_to_all | solution.py:60
  61.1 26.6 %all-to-all-start.2 = ((f32[16,8,648]{2,1,0:T(8,128)}), f32[16,8,648]{2,1,0:T(8,128)}, u32[]{:S(2)}, u32[]{:S(2)}) async-start(f32[16,8,648]{2,1,0:T(8,128)} %maximum_bitcast_fusion), calls=%async_computation.2 | async-start | bytes 786432 | tf_op jit(solution)/shard_map/all_to_all | solution.py:97
  129.5 25.7 %all-to-all-start.3 = ((bf16[32,2,1,2,8,128]{5,4,3,1,2,0:T(8,128)(2,1)}), bf16[32,2,1,2,8,128]{5,4,3,1,2,0:T(8,128)(2,1)}, u32[]{:S(2)}, u32[]{:S(2)}) async-start(bf16[32,2,1,2,8,128]{5,4,3,1,2,0:T(8,128)(2,1)} %bitcast.112), calls=%async_computation.3 | async-start | bytes 524288 | tf_op jit(solution)/shard_map/all_to_all | solution.py:148
  155.2 2.5 %copy-start.5 = (bf16[8,8192]{1,0:T(8,128)(2,1)S(1)}, bf16[8,8192]{1,0:T(8,128)(2,1)}, u32[]{:S(2)}) copy-start(bf16[8,8192]{1,0:T(8,128)(2,1)} %all_gather.3) | copy-start | bytes 393220
where the time goes:
time: 160 us; the launch traced here: 158 us
  starting transfers between devices  48.7 us (30%)
  local copies, waits for them, and re-layouts  32.1 us (20%)
  blocking collectives  28.5 us (18%)
  waiting for transfers between devices  23.2 us (14%)
  other arithmetic  20.9 us (13%)
  matrix products  4.13 us (3%)
    all_gather x1, blocking collectives, shards(): attention = lax.all_gather(own_attention, 'grp', axis=1, tiled=True)  28.5 us
    all_to_all x1, starting transfers between devices, shards(): lax.all_to_all(outbound, 'req', split_axis=0, concat_axis=0, tiled=True)  16.8 us
    all_to_all x1, starting transfers between devices, shards(): lax.all_to_all(jnp.broadcast_to(mid_owned[None], (groups,) + mid_owned.sh...  12.5 us
    all_to_all x1, starting transfers between devices, shards(): summed = jnp.sum(lax.all_to_all(partial, 'req', 0, 0, tiled=False), axis=0)  11 us
    all_to_all x1, waiting for transfers between devices, shards(): received = lax.all_to_all(parcel, 'grp', 0, 0, tiled=False)  10.9 us
    all_to_all x1, starting transfers between devices, shards(): received = lax.all_to_all(parcel, 'grp', 0, 0, tiled=False)  8.38 us
    all_to_all x1, waiting for transfers between devices, shards(): lax.all_to_all(outbound, 'req', split_axis=0, concat_axis=0, tiled=True)  7.77 us
    unnamed x29, local copies, waits for them, and re-layouts  4.87 us
  transfers between devices with their start and end apart: 4, of which 4 were waited for; matrix products, arithmetic and copies ran while one was open for 15% of the time, Pallas kernels for 0%

commit v1 on v0

--- a/solution.py
+++ b/solution.py
@@ -6,6 +6,29 @@
 
 adapter_scale = 2.0
 masked_score = -1e30
+
+
+def supply_all_sections(vals, axis_name):
+    lower = lax.axis_size(axis_name)
+    block_now = lax.axis_index(axis_name)
+    parts_out, newest, k_now = (lower, block_now, vals.shape[1])
+    sheets = [(u, (u + 1) % parts_out) for u in range(parts_out)]
+    by_rank = [(u, (u - 1) % parts_out) for u in range(parts_out)]
+    moved = jnp.zeros((*vals.shape[:1], parts_out * k_now, *vals.shape[2:]), vals.dtype)
+    moved = lax.dynamic_update_slice_in_dim(moved, vals, newest * k_now, axis=1)
+    x_now = n_now = vals
+    y = parts_out // 2
+    for k in range(1, y + 1):
+        x_now = lax.ppermute(x_now, axis_name, sheets)
+        moved = lax.dynamic_update_slice_in_dim(
+            moved, x_now, (newest - k) % parts_out * k_now, axis=1
+        )
+        if k < parts_out - y:
+            n_now = lax.ppermute(n_now, axis_name, by_rank)
+            moved = lax.dynamic_update_slice_in_dim(
+                moved, n_now, (newest + k) % parts_out * k_now, axis=1
+            )
+    return moved
 
 
 def shards(
@@ -123,7 +146,7 @@
         + new_weight[..., None] * own_value.astype(jnp.float32)[:, None, :]
     )
     own_attention = (mixed / total[..., None]).astype(jnp.bfloat16).reshape(rows, mixed_width)
-    attention = lax.all_gather(own_attention, "grp", axis=1, tiled=True)
+    attention = supply_all_sections(own_attention, "grp")
     page_slot = page_slot_table[request_index, lengths // page_size]
     offset = lengths % page_size
     mine = offset // slot_tokens == group_index

time: 160 us -> 182 us (1.14)
  the two profiles are of different devices: /device:TPU:1 before, /device:TPU:2 now
where the time goes in v1:
time: 182 us; the launch traced here: 181 us
  starting transfers between devices  87.2 us (48%)
  local copies, waits for them, and re-layouts  38.8 us (21%)
  waiting for transfers between devices  33.9 us (19%)
  other arithmetic  16.2 us (9%)
  matrix products  3.03 us (2%)
    ppermute x7, starting transfers between devices, supply_all_sections(): n_now = lax.ppermute(n_now, axis_name, by_rank)  34.9 us
    all_to_all x1, waiting for transfers between devices, shards(): received = lax.all_to_all(parcel, 'grp', 0, 0, tiled=False)  18.3 us
    ppermute x8, starting transfers between devices, supply_all_sections(): x_now = lax.ppermute(x_now, axis_name, sheets)  17.7 us
    all_to_all x1, starting transfers between devices, shards(): lax.all_to_all(jnp.broadcast_to(mid_owned[None], (groups,) + mid_owned.sh...  12.9 us
    all_to_all x1, waiting for transfers between devices, shards(): lax.all_to_all(jnp.broadcast_to(mid_owned[None], (groups,) + mid_owned.sh...  11.9 us
    all_to_all x1, starting transfers between devices, shards(): summed = jnp.sum(lax.all_to_all(partial, 'req', 0, 0, tiled=False), axis=0)  10.1 us
    all_to_all x1, starting transfers between devices, shards(): lax.all_to_all(outbound, 'req', split_axis=0, concat_axis=0, tiled=True)  7.33 us
    dynamic_update_slice x8, local copies, waits for them, and re-layouts, supply_all_sections(): lax.dynamic_update_slice_in_dim(moved, x_now, (newest - k) % parts_out *...  5.54 us
  transfers between devices with their start and end apart: 19, of which 3 were waited for; matrix products, arithmetic and copies ran while one was open for 19% of the time, Pallas kernels for 0%

profile of v1, /device:TPU:2, one launch (start us, length us, event | category | flops | bytes accessed | tf_op | source)
XLA Modules:
  0.0 180.5 jit_solution(752614731723997810)
XLA Ops:
  9.7 10.1 %all-to-all-start = ((f32[32,8,256]{2,1,0:T(8,128)}), f32[32,8,256]{2,1,0:T(8,128)}, u32[]{:S(2)}, u32[]{:S(2)}) async-start(f32[32,8,256]{2,1,0:T(8,128)} %bitcast.117), calls=%async_computation | async-start | bytes 524288 | tf_op jit(solution)/shard_map/all_to_all | solution.py:78
  33.1 12.9 %all-to-all-start.1 = ((bf16[16,8,128]{2,1,0:T(8,128)(2,1)}), bf16[16,8,128]{2,1,0:T(8,128)(2,1)}, u32[]{:S(2)}, u32[]{:S(2)}) async-start(bf16[16,8,128]{2,1,0:T(8,128)(2,1)} %broadcast_in_dim.48), calls=%async_computation.1 | async-start | bytes 65536 | tf_op jit(solution)/shard_map/all_to_all | solution.py:83
  46.7 11.9 %all-to-all-done.1 = bf16[16,8,128]{2,1,0:T(8,128)(2,1)} async-done(((bf16[16,8,128]{2,1,0:T(8,128)(2,1)}), bf16[16,8,128]{2,1,0:T(8,128)(2,1)}, u32[]{:S(2)}, u32[]{:S(2)}) %all-to-all-start.1) | async-done | bytes 32800 | tf_op jit(solution)/shard_map/all_to_all | solution.py:83
  61.8 1.8 %maximum_bitcast_fusion = f32[16,8,648]{2,1,0:T(8,128)} fusion(f32[8,16,128]{2,0,1:T(8,128)S(1)} %broadcast_in_dim.49, f32[8,16,4]{2,0,1:T(8,128)S(1)} %copy.46, f32[8,16,4]{2,0,1:T(8,128)S(1)} %copy.45, f32[8,16,512]{2,0,1:T(8,128)} %copy.44), kind=kLoop, calls=%fused_computation.22 | loop fusion | flops 248832 | bytes 663552 | tf_op jit(solution)/shard_map/transpose | solution.py:119
  63.6 4.3 %all-to-all-start.2 = ((f32[16,8,648]{2,1,0:T(8,128)}), f32[16,8,648]{2,1,0:T(8,128)}, u32[]{:S(2)}, u32[]{:S(2)}) async-start(f32[16,8,648]{2,1,0:T(8,128)} %maximum_bitcast_fusion), calls=%async_computation.2 | async-start | bytes 786432 | tf_op jit(solution)/shard_map/all_to_all | solution.py:120
  72.1 18.3 %all-to-all-done.2 = f32[16,8,648]{2,1,0:T(8,128)} async-done(((f32[16,8,648]{2,1,0:T(8,128)}), f32[16,8,648]{2,1,0:T(8,128)}, u32[]{:S(2)}, u32[]{:S(2)}) %all-to-all-start.2) | async-done | bytes 331808 | tf_op jit(solution)/shard_map/all_to_all | solution.py:120
  97.4 4.4 %collective-permute-start = (bf16[8,512]{1,0:T(8,128)(2,1)}, bf16[8,512]{1,0:T(8,128)(2,1)}, u32[]{:S(2)}, u32[]{:S(2)}) collective-permute-start(bf16[8,512]{1,0:T(8,128)(2,1)} %get-tuple-element.3), channel_id=1, source_target_pairs={{0,1},{1,2},{2,3},{3,4},{4,5},{5,6},{6,7},{7,8},{8,9},{9,10},{10,1... | collective-permute-start | bytes 24584 | tf_op jit(solution)/shard_map/ppermute | solution.py:22
  101.7 4.1 %collective-permute-start.1 = (bf16[8,512]{1,0:T(8,128)(2,1)}, bf16[8,512]{1,0:T(8,128)(2,1)S(1)}, u32[]{:S(2)}, u32[]{:S(2)}) collective-permute-start(bf16[8,512]{1,0:T(8,128)(2,1)} %get-tuple-element.3), channel_id=1, source_target_pairs={{0,15},{1,0},{2,1},{3,2},{4,3},{5,4},{6,5},{7,6},{8,7},{9,8},{10,9... | collective-permute-start | bytes 24584 | tf_op jit(solution)/shard_map/ppermute | solution.py:27
  110.7 3.6 %scatter_fusion.1 = bf16[32,2,2,8,128]{4,3,2,1,0:T(8,128)(2,1)} fusion(bf16[32,2,2,8,128]{4,3,2,1,0:T(8,128)(2,1)} %broadcast.243, s32[32]{0:T(128)S(1)} %fusion.39, bf16[32,2,8,128]{3,2,1,0:T(8,128)(2,1)S(1)} %gather_fusion.5), kind=kCustom, calls=%fused_computation.7 | custom fusion | bytes 393472 | tf_op jit(solution)/shard_map/scatter | solution.py:169
  114.3 7.3 %all-to-all-start.3 = ((bf16[32,2,1,2,8,128]{5,4,3,1,2,0:T(8,128)(2,1)}), bf16[32,2,1,2,8,128]{5,4,3,1,2,0:T(8,128)(2,1)S(1)}, u32[]{:S(2)}, u32[]{:S(2)}) async-start(bf16[32,2,1,2,8,128]{5,4,3,1,2,0:T(8,128)(2,1)} %bitcast.41), calls=%async_computation.3 | async-start | bytes 524288 | tf_op jit(solution)/shard_map/all_to_all | solution.py:171
  121.6 1.9 %collective-permute-start.2 = (bf16[8,512]{1,0:T(8,128)(2,1)}, bf16[8,512]{1,0:T(8,128)(2,1)S(1)}, u32[]{:S(2)}, u32[]{:S(2)}) collective-permute-start(bf16[8,512]{1,0:T(8,128)(2,1)} %collective-permute-done), channel_id=1, source_target_pairs={{0,1},{1,2},{2,3},{3,4},{4,5},{5,6},{6,7},{7,8},{8,9},{9,10},{10,1... | collective-permute-start | bytes 24584 | tf_op jit(solution)/shard_map/ppermute | solution.py:22
  123.6 5.1 %collective-permute-start.3 = (bf16[8,512]{1,0:T(8,128)(2,1)S(1)}, bf16[8,512]{1,0:T(8,128)(2,1)S(1)}, u32[]{:S(2)}, u32[]{:S(2)}) collective-permute-start(bf16[8,512]{1,0:T(8,128)(2,1)S(1)} %collective-permute-done.1), channel_id=1, source_target_pairs={{0,15},{1,0},{2,1},{3,2},{4,3},{5,4},{6,5},{7,6},{8,7},{9,8},{10,9... | collective-permute-start | bytes 24584 | tf_op jit(solution)/shard_map/ppermute | solution.py:27
  130.6 1.9 %collective-permute-start.4 = (bf16[8,512]{1,0:T(8,128)(2,1)S(1)}, bf16[8,512]{1,0:T(8,128)(2,1)S(1)}, u32[]{:S(2)}, u32[]{:S(2)}) collective-permute-start(bf16[8,512]{1,0:T(8,128)(2,1)S(1)} %collective-permute-done.2), channel_id=1, source_target_pairs={{0,1},{1,2},{2,3},{3,4},{4,5},{5,6},{6,7},{7,8},{8,9},{9,10},{10,1... | collective-permute-start | bytes 24584 | tf_op jit(solution)/shard_map/ppermute | solution.py:22
  132.5 5.1 %collective-permute-start.5 = (bf16[8,512]{1,0:T(8,128)(2,1)S(1)}, bf16[8,512]{1,0:T(8,128)(2,1)S(1)}, u32[]{:S(2)}, u32[]{:S(2)}) collective-permute-start(bf16[8,512]{1,0:T(8,128)(2,1)S(1)} %collective-permute-done.3), channel_id=1, source_target_pairs={{0,15},{1,0},{2,1},{3,2},{4,3},{5,4},{6,5},{7,6},{8,7},{9,8},{10,9... | collective-permute-start | bytes 24584 | tf_op jit(solution)/shard_map/ppermute | solution.py:27
  138.9 1.9 %collective-permute-start.6 = (bf16[8,512]{1,0:T(8,128)(2,1)S(1)}, bf16[8,512]{1,0:T(8,128)(2,1)S(1)}, u32[]{:S(2)}, u32[]{:S(2)}) collective-permute-start(bf16[8,512]{1,0:T(8,128)(2,1)S(1)} %collective-permute-done.4), channel_id=1, source_target_pairs={{0,1},{1,2},{2,3},{3,4},{4,5},{5,6},{6,7},{7,8},{8,9},{9,10},{10,1... | collective-permute-start | bytes 24584 | tf_op jit(solution)/shard_map/ppermute | solution.py:22
  140.8 5.1 %collective-permute-start.7 = (bf16[8,512]{1,0:T(8,128)(2,1)S(1)}, bf16[8,512]{1,0:T(8,128)(2,1)S(1)}, u32[]{:S(2)}, u32[]{:S(2)}) collective-permute-start(bf16[8,512]{1,0:T(8,128)(2,1)S(1)} %collective-permute-done.5), channel_id=1, source_target_pairs={{0,15},{1,0},{2,1},{3,2},{4,3},{5,4},{6,5},{7,6},{8,7},{9,8},{10,9... | collective-permute-start | bytes 24584 | tf_op jit(solution)/shard_map/ppermute | solution.py:27
  147.2 1.9 %collective-permute-start.8 = (bf16[8,512]{1,0:T(8,128)(2,1)S(1)}, bf16[8,512]{1,0:T(8,128)(2,1)S(1)}, u32[]{:S(2)}, u32[]{:S(2)}) collective-permute-start(bf16[8,512]{1,0:T(8,128)(2,1)S(1)} %collective-permute-done.6), channel_id=1, source_target_pairs={{0,1},{1,2},{2,3},{3,4},{4,5},{5,6},{6,7},{7,8},{8,9},{9,10},{10,1... | collective-permute-start | bytes 24584 | tf_op jit(solution)/shard_map/ppermute | solution.py:22
  149.1 5.1 %collective-permute-start.9 = (bf16[8,512]{1,0:T(8,128)(2,1)S(1)}, bf16[8,512]{1,0:T(8,128)(2,1)S(1)}, u32[]{:S(2)}, u32[]{:S(2)}) collective-permute-start(bf16[8,512]{1,0:T(8,128)(2,1)S(1)} %collective-permute-done.7), channel_id=1, source_target_pairs={{0,15},{1,0},{2,1},{3,2},{4,3},{5,4},{6,5},{7,6},{8,7},{9,8},{10,9... | collective-permute-start | bytes 24584 | tf_op jit(solution)/shard_map/ppermute | solution.py:27
  155.4 1.9 %collective-permute-start.10 = (bf16[8,512]{1,0:T(8,128)(2,1)S(1)}, bf16[8,512]{1,0:T(8,128)(2,1)S(1)}, u32[]{:S(2)}, u32[]{:S(2)}) collective-permute-start(bf16[8,512]{1,0:T(8,128)(2,1)S(1)} %collective-permute-done.8), channel_id=1, source_target_pairs={{0,1},{1,2},{2,3},{3,4},{4,5},{5,6},{6,7},{7,8},{8,9},{9,10},{10,1... | collective-permute-start | bytes 24584 | tf_op jit(solution)/shard_map/ppermute | solution.py:22
  157.4 5.1 %collective-permute-start.11 = (bf16[8,512]{1,0:T(8,128)(2,1)S(1)}, bf16[8,512]{1,0:T(8,128)(2,1)S(1)}, u32[]{:S(2)}, u32[]{:S(2)}) collective-permute-start(bf16[8,512]{1,0:T(8,128)(2,1)S(1)} %collective-permute-done.9), channel_id=1, source_target_pairs={{0,15},{1,0},{2,1},{3,2},{4,3},{5,4},{6,5},{7,6},{8,7},{9,8},{10,9... | collective-permute-start | bytes 24584 | tf_op jit(solution)/shard_map/ppermute | solution.py:27
  163.7 1.9 %collective-permute-start.12 = (bf16[8,512]{1,0:T(8,128)(2,1)S(1)}, bf16[8,512]{1,0:T(8,128)(2,1)S(1)}, u32[]{:S(2)}, u32[]{:S(2)}) collective-permute-start(bf16[8,512]{1,0:T(8,128)(2,1)S(1)} %collective-permute-done.10), channel_id=1, source_target_pairs={{0,1},{1,2},{2,3},{3,4},{4,5},{5,6},{6,7},{7,8},{8,9},{9,10},{10,1... | collective-permute-start | bytes 24584 | tf_op jit(solution)/shard_map/ppermute | solution.py:22
  165.6 5.1 %collective-permute-start.13 = (bf16[8,512]{1,0:T(8,128)(2,1)S(1)}, bf16[8,512]{1,0:T(8,128)(2,1)S(1)}, u32[]{:S(2)}, u32[]{:S(2)}) collective-permute-start(bf16[8,512]{1,0:T(8,128)(2,1)S(1)} %collective-permute-done.11), channel_id=1, source_target_pairs={{0,15},{1,0},{2,1},{3,2},{4,3},{5,4},{6,5},{7,6},{8,7},{9,8},{10,9... | collective-permute-start | bytes 24584 | tf_op jit(solution)/shard_map/ppermute | solution.py:27
  172.0 1.9 %collective-permute-start.14 = (bf16[8,512]{1,0:T(8,128)(2,1)S(1)}, bf16[8,512]{1,0:T(8,128)(2,1)S(1)}, u32[]{:S(2)}, u32[]{:S(2)}) collective-permute-start(bf16[8,512]{1,0:T(8,128)(2,1)S(1)} %collective-permute-done.12), channel_id=1, source_target_pairs={{0,1},{1,2},{2,3},{3,4},{4,5},{5,6},{6,7},{7,8},{8,9},{9,10},{10,1... | collective-permute-start | bytes 24584 | tf_op jit(solution)/shard_map/ppermute | solution.py:22
  175.1 3.6 %collective-permute-done.14 = bf16[8,512]{1,0:T(8,128)(2,1)S(1)} collective-permute-done((bf16[8,512]{1,0:T(8,128)(2,1)S(1)}, bf16[8,512]{1,0:T(8,128)(2,1)S(1)}, u32[]{:S(2)}, u32[]{:S(2)}) %collective-permute-start.14) | collective-permute-done | bytes 8224 | tf_op jit(solution)/shard_map/ppermute | solution.py:22
  (132 shorter events, 52.6 us)
Async XLA Ops:
  0.6 29.6 %copy-start = (bf16[128,64,128]{2,1,0:T(8,128)(2,1)S(1)}, bf16[128,64,128]{2,1,0:T(8,128)(2,1)}, u32[]{:S(2)}) copy-start(bf16[128,64,128]{2,1,0:T(8,128)(2,1)} %param.14) | copy-start | bytes 6291460
  5.8 13.9 %copy-start.1 = (s32[8,32]{1,0:T(8,128)S(1)}, s32[8,32]{1,0:T(8,128)}, u32[]{:S(2)}) copy-start(s32[8,32]{1,0:T(8,128)} %param.19) | copy-start | bytes 3076
  9.7 21.8 %all-to-all-start = ((f32[32,8,256]{2,1,0:T(8,128)}), f32[32,8,256]{2,1,0:T(8,128)}, u32[]{:S(2)}, u32[]{:S(2)}) async-start(f32[32,8,256]{2,1,0:T(8,128)} %bitcast.117), calls=%async_computation | async-start | bytes 524288 | tf_op jit(solution)/shard_map/all_to_all | solution.py:78
  33.1 25.5 %all-to-all-start.1 = ((bf16[16,8,128]{2,1,0:T(8,128)(2,1)}), bf16[16,8,128]{2,1,0:T(8,128)(2,1)}, u32[]{:S(2)}, u32[]{:S(2)}) async-start(bf16[16,8,128]{2,1,0:T(8,128)(2,1)} %broadcast_in_dim.48), calls=%async_computation.1 | async-start | bytes 65536 | tf_op jit(solution)/shard_map/all_to_all | solution.py:83
  61.8 9.8 %copy-start.12 = (s32[8]{0:T(128)S(1)}, s32[8]{0:T(128)}, u32[]{:S(2)}) copy-start(s32[8]{0:T(128)} %param.18) | copy-start | bytes 100
  63.6 26.7 %all-to-all-start.2 = ((f32[16,8,648]{2,1,0:T(8,128)}), f32[16,8,648]{2,1,0:T(8,128)}, u32[]{:S(2)}, u32[]{:S(2)}) async-start(f32[16,8,648]{2,1,0:T(8,128)} %maximum_bitcast_fusion), calls=%async_computation.2 | async-start | bytes 786432 | tf_op jit(solution)/shard_map/all_to_all | solution.py:120
  97.4 9.9 %copy-start.5 = (bf16[8,8192]{1,0:T(8,128)(2,1)}, bf16[8,8192]{1,0:T(8,128)(2,1)S(1)}, u32[]{:S(2)}) copy-start(bf16[8,8192]{1,0:T(8,128)(2,1)S(1)} %get-tuple-element.2) | copy-start | bytes 393220
  97.4 24.3 %collective-permute-start = (bf16[8,512]{1,0:T(8,128)(2,1)}, bf16[8,512]{1,0:T(8,128)(2,1)}, u32[]{:S(2)}, u32[]{:S(2)}) collective-permute-start(bf16[8,512]{1,0:T(8,128)(2,1)} %get-tuple-element.3), channel_id=1, source_target_pairs={{0,1},{1,2},{2,3},{3,4},{4,5},{5,6},{6,7},{7,8},{8,9},{9,10},{10,1... | collective-permute-start | bytes 24584 | tf_op jit(solution)/shard_map/ppermute | solution.py:22
  101.7 21.8 %collective-permute-start.1 = (bf16[8,512]{1,0:T(8,128)(2,1)}, bf16[8,512]{1,0:T(8,128)(2,1)S(1)}, u32[]{:S(2)}, u32[]{:S(2)}) collective-permute-start(bf16[8,512]{1,0:T(8,128)(2,1)} %get-tuple-element.3), channel_id=1, source_target_pairs={{0,15},{1,0},{2,1},{3,2},{4,3},{5,4},{6,5},{7,6},{8,7},{9,8},{10,9... | collective-permute-start | bytes 24584 | tf_op jit(solution)/shard_map/ppermute | solution.py:27
  110.0 69.4 %copy-start.3 = (bf16[256,1,2,8,128]{4,3,2,1,0:T(8,128)(2,1)S(1)}, bf16[256,1,2,8,128]{4,3,2,1,0:T(8,128)(2,1)}, u32[]{:S(2)}) copy-start(bf16[256,1,2,8,128]{4,3,2,1,0:T(8,128)(2,1)} %slice_bitcast_fusion) | copy-start | bytes 3145732
  114.3 65.1 %all-to-all-start.3 = ((bf16[32,2,1,2,8,128]{5,4,3,1,2,0:T(8,128)(2,1)}), bf16[32,2,1,2,8,128]{5,4,3,1,2,0:T(8,128)(2,1)S(1)}, u32[]{:S(2)}, u32[]{:S(2)}) async-start(bf16[32,2,1,2,8,128]{5,4,3,1,2,0:T(8,128)(2,1)} %bitcast.41), calls=%async_computation.3 | async-start | bytes 524288 | tf_op jit(solution)/shard_map/all_to_all | solution.py:171
  121.6 9.0 %collective-permute-start.2 = (bf16[8,512]{1,0:T(8,128)(2,1)}, bf16[8,512]{1,0:T(8,128)(2,1)S(1)}, u32[]{:S(2)}, u32[]{:S(2)}) collective-permute-start(bf16[8,512]{1,0:T(8,128)(2,1)} %collective-permute-done), channel_id=1, source_target_pairs={{0,1},{1,2},{2,3},{3,4},{4,5},{5,6},{6,7},{7,8},{8,9},{9,10},{10,1... | collective-permute-start | bytes 24584 | tf_op jit(solution)/shard_map/ppermute | solution.py:22
  123.6 9.0 %collective-permute-start.3 = (bf16[8,512]{1,0:T(8,128)(2,1)S(1)}, bf16[8,512]{1,0:T(8,128)(2,1)S(1)}, u32[]{:S(2)}, u32[]{:S(2)}) collective-permute-start(bf16[8,512]{1,0:T(8,128)(2,1)S(1)} %collective-permute-done.1), channel_id=1, source_target_pairs={{0,15},{1,0},{2,1},{3,2},{4,3},{5,4},{6,5},{7,6},{8,7},{9,8},{10,9... | collective-permute-start | bytes 24584 | tf_op jit(solution)/shard_map/ppermute | solution.py:27
  130.6 8.3 %collective-permute-start.4 = (bf16[8,512]{1,0:T(8,128)(2,1)S(1)}, bf16[8,512]{1,0:T(8,128)(2,1)S(1)}, u32[]{:S(2)}, u32[]{:S(2)}) collective-permute-start(bf16[8,512]{1,0:T(8,128)(2,1)S(1)} %collective-permute-done.2), channel_id=1, source_target_pairs={{0,1},{1,2},{2,3},{3,4},{4,5},{5,6},{6,7},{7,8},{8,9},{9,10},{10,1... | collective-permute-start | bytes 24584 | tf_op jit(solution)/shard_map/ppermute | solution.py:22
  132.5 8.3 %collective-permute-start.5 = (bf16[8,512]{1,0:T(8,128)(2,1)S(1)}, bf16[8,512]{1,0:T(8,128)(2,1)S(1)}, u32[]{:S(2)}, u32[]{:S(2)}) collective-permute-start(bf16[8,512]{1,0:T(8,128)(2,1)S(1)} %collective-permute-done.3), channel_id=1, source_target_pairs={{0,15},{1,0},{2,1},{3,2},{4,3},{5,4},{6,5},{7,6},{8,7},{9,8},{10,9... | collective-permute-start | bytes 24584 | tf_op jit(solution)/shard_map/ppermute | solution.py:27
  138.9 8.3 %collective-permute-start.6 = (bf16[8,512]{1,0:T(8,128)(2,1)S(1)}, bf16[8,512]{1,0:T(8,128)(2,1)S(1)}, u32[]{:S(2)}, u32[]{:S(2)}) collective-permute-start(bf16[8,512]{1,0:T(8,128)(2,1)S(1)} %collective-permute-done.4), channel_id=1, source_target_pairs={{0,1},{1,2},{2,3},{3,4},{4,5},{5,6},{6,7},{7,8},{8,9},{9,10},{10,1... | collective-permute-start | bytes 24584 | tf_op jit(solution)/shard_map/ppermute | solution.py:22
  140.8 8.3 %collective-permute-start.7 = (bf16[8,512]{1,0:T(8,128)(2,1)S(1)}, bf16[8,512]{1,0:T(8,128)(2,1)S(1)}, u32[]{:S(2)}, u32[]{:S(2)}) collective-permute-start(bf16[8,512]{1,0:T(8,128)(2,1)S(1)} %collective-permute-done.5), channel_id=1, source_target_pairs={{0,15},{1,0},{2,1},{3,2},{4,3},{5,4},{6,5},{7,6},{8,7},{9,8},{10,9... | collective-permute-start | bytes 24584 | tf_op jit(solution)/shard_map/ppermute | solution.py:27
  147.2 8.3 %collective-permute-start.8 = (bf16[8,512]{1,0:T(8,128)(2,1)S(1)}, bf16[8,512]{1,0:T(8,128)(2,1)S(1)}, u32[]{:S(2)}, u32[]{:S(2)}) collective-permute-start(bf16[8,512]{1,0:T(8,128)(2,1)S(1)} %collective-permute-done.6), channel_id=1, source_target_pairs={{0,1},{1,2},{2,3},{3,4},{4,5},{5,6},{6,7},{7,8},{8,9},{9,10},{10,1... | collective-permute-start | bytes 24584 | tf_op jit(solution)/shard_map/ppermute | solution.py:22
  149.1 8.3 %collective-permute-start.9 = (bf16[8,512]{1,0:T(8,128)(2,1)S(1)}, bf16[8,512]{1,0:T(8,128)(2,1)S(1)}, u32[]{:S(2)}, u32[]{:S(2)}) collective-permute-start(bf16[8,512]{1,0:T(8,128)(2,1)S(1)} %collective-permute-done.7), channel_id=1, source_target_pairs={{0,15},{1,0},{2,1},{3,2},{4,3},{5,4},{6,5},{7,6},{8,7},{9,8},{10,9... | collective-permute-start | bytes 24584 | tf_op jit(solution)/shard_map/ppermute | solution.py:27
  155.4 8.3 %collective-permute-start.10 = (bf16[8,512]{1,0:T(8,128)(2,1)S(1)}, bf16[8,512]{1,0:T(8,128)(2,1)S(1)}, u32[]{:S(2)}, u32[]{:S(2)}) collective-permute-start(bf16[8,512]{1,0:T(8,128)(2,1)S(1)} %collective-permute-done.8), channel_id=1, source_target_pairs={{0,1},{1,2},{2,3},{3,4},{4,5},{5,6},{6,7},{7,8},{8,9},{9,10},{10,1... | collective-permute-start | bytes 24584 | tf_op jit(solution)/shard_map/ppermute | solution.py:22
  157.4 8.3 %collective-permute-start.11 = (bf16[8,512]{1,0:T(8,128)(2,1)S(1)}, bf16[8,512]{1,0:T(8,128)(2,1)S(1)}, u32[]{:S(2)}, u32[]{:S(2)}) collective-permute-start(bf16[8,512]{1,0:T(8,128)(2,1)S(1)} %collective-permute-done.9), channel_id=1, source_target_pairs={{0,15},{1,0},{2,1},{3,2},{4,3},{5,4},{6,5},{7,6},{8,7},{9,8},{10,9... | collective-permute-start | bytes 24584 | tf_op jit(solution)/shard_map/ppermute | solution.py:27
  163.7 8.3 %collective-permute-start.12 = (bf16[8,512]{1,0:T(8,128)(2,1)S(1)}, bf16[8,512]{1,0:T(8,128)(2,1)S(1)}, u32[]{:S(2)}, u32[]{:S(2)}) collective-permute-start(bf16[8,512]{1,0:T(8,128)(2,1)S(1)} %collective-permute-done.10), channel_id=1, source_target_pairs={{0,1},{1,2},{2,3},{3,4},{4,5},{5,6},{6,7},{7,8},{8,9},{9,10},{10,1... | collective-permute-start | bytes 24584 | tf_op jit(solution)/shard_map/ppermute | solution.py:22
  165.6 8.9 %collective-permute-start.13 = (bf16[8,512]{1,0:T(8,128)(2,1)S(1)}, bf16[8,512]{1,0:T(8,128)(2,1)S(1)}, u32[]{:S(2)}, u32[]{:S(2)}) collective-permute-start(bf16[8,512]{1,0:T(8,128)(2,1)S(1)} %collective-permute-done.11), channel_id=1, source_target_pairs={{0,15},{1,0},{2,1},{3,2},{4,3},{5,4},{6,5},{7,6},{8,7},{9,8},{10,9... | collective-permute-start | bytes 24584 | tf_op jit(solution)/shard_map/ppermute | solution.py:27
  172.0 6.7 %collective-permute-start.14 = (bf16[8,512]{1,0:T(8,128)(2,1)S(1)}, bf16[8,512]{1,0:T(8,128)(2,1)S(1)}, u32[]{:S(2)}, u32[]{:S(2)}) collective-permute-start(bf16[8,512]{1,0:T(8,128)(2,1)S(1)} %collective-permute-done.12), channel_id=1, source_target_pairs={{0,1},{1,2},{2,3},{3,4},{4,5},{5,6},{6,7},{7,8},{8,9},{9,10},{10,1... | collective-permute-start | bytes 24584 | tf_op jit(solution)/shard_map/ppermute | solution.py:22
  (11 other events, 28.4 us)
